TPU v7x, 256 devices: a whole 4x4x8 slice. The times are simulated.
256 devices in a mesh: src: 16 (over y, x), tgt: 16 (over z, core).
Axes of the slice: x: 4, y: 4, z: 8, core: 2. Of those that a mesh axis runs over, the one named last changes fastest.
Arguments:
- src_emb_t: bfloat16 [300, 16384], P(None, 'src'), may hold values from -6 to 6
- tgt_emb_t: bfloat16 [300, 32768], P(None, 'tgt'), may hold values from -6 to 6
- core: float32 [300, 300], replicated, may hold values from -0.08 to 0.2
- src_logw: float32 [16384], P('src'), may hold values from -1.5 to 1.5
- tgt_logw: float32 [32768], P('tgt'), may hold values from -1.5 to 1.5
Outputs:
- src_potential: float32 [16384], P('src')
- tgt_potential: float32 [32768], P('tgt')
- next_core: float32 [300, 300], replicated
All inputs are finite; a program needn't handle non-finite values.
Results may differ from a plain program's by a relative error of at most 0.0036.
Values sent between devices are 32-bit elements; how exact they have to be, the bound alone decides.
No kernel may reach another device: no remote copies, remote signals or barrier semaphores. Data moves between devices by JAX's collectives and lax.ppermute only.
A program may use at most 64 MiB of HBM per device.

v0:
```python
import jax
import jax.numpy as jnp
from jax import lax
from jax.sharding import PartitionSpec as P

D = 300
ITERS = 3


def row_lse(shifted):
    peaks = jnp.max(shifted, axis=1)
    peaks = lax.pmax(peaks, "tgt")
    totals = lax.psum(jnp.sum(jnp.exp(shifted - peaks[:, None]), axis=1), "tgt")
    return peaks + jnp.log(totals)


def col_lse(shifted):
    peaks = jnp.max(shifted, axis=0)
    peaks = lax.pmax(peaks, "src")
    totals = lax.psum(jnp.sum(jnp.exp(shifted - peaks[None, :]), axis=0), "src")
    return peaks + jnp.log(totals)


def per_device(src_emb_t, tgt_emb_t, core, src_logw, tgt_logw):
    projected = jnp.dot(
        core.T, src_emb_t.astype(jnp.float32), precision=lax.Precision.HIGHEST
    ).astype(jnp.bfloat16)

    def scores_of():
        return lax.dot_general(
            projected, tgt_emb_t, (((0,), (0,)), ((), ())), preferred_element_type=jnp.float32
        )

    stored = scores_of()
    tgt_pot = jnp.zeros((tgt_emb_t.shape[1],), jnp.float32)
    src_pot = jnp.zeros((src_emb_t.shape[1],), jnp.float32)
    for step in range(ITERS):
        current = stored if step == 0 else scores_of()
        src_pot = src_logw - row_lse(current + tgt_pot[None, :])
        current = scores_of()
        tgt_pot = tgt_logw - col_lse(current + src_pot[:, None])
    current = scores_of()
    plan = jnp.exp(current + src_pot[:, None] + tgt_pot[None, :]).astype(jnp.bfloat16)
    total_words = src_emb_t.shape[1] * lax.axis_size("src")
    share = src_emb_t.shape[1] // lax.axis_size("tgt")
    portion = lax.psum_scatter(
        lax.dot_general(
            plan, tgt_emb_t, (((1,), (1,)), ((), ())), preferred_element_type=jnp.float32
        ),
        "tgt",
        scatter_dimension=0,
        tiled=True,
    )
    offset = lax.axis_index("tgt") * share
    my_words = lax.dynamic_slice_in_dim(src_emb_t, offset, share, 1)
    partial_core = jnp.dot(my_words.astype(jnp.float32), portion, precision=lax.Precision.HIGHEST)
    summed = lax.psum(partial_core, ("src", "tgt"))
    next_core = summed * (D / total_words)
    return (src_pot, tgt_pot, next_core)


def solution(mesh):
    placed = (P(None, "src"), P(None, "tgt"), P(), P("src"), P("tgt"))
    return jax.shard_map(
        per_device, mesh=mesh, in_specs=placed, out_specs=(P("src"), P("tgt"), P()), check_vma=False
    )
```

profile of v0, /device:TPU:2, one launch (start us, length us, event | category | flops | bytes accessed | tf_op | source)
XLA Modules:
  0.0 762.6 jit_solution(15984662700582594350)
XLA Ops:
  9.7 5.6 fusion.6
  15.4 28.8 %pmax.42 = f32[1024]{0:T(1024)S(1)} all-reduce(f32[1024]{0:T(1024)S(1)} %get-tuple-element.3), channel_id=1, replica_groups=mesh['src'=16,'tgt'=16] {'tgt'}, use_global_device_ids=true, to_apply=%region_1.0 | all-reduce | flops 1024 | bytes 8192 | tf_op jit(solution)/shard_map/pmax | solution.py:12
  44.2 4.6 exponential_reduce_fusion.5
  48.8 23.6 %psum.49 = f32[1024]{0:T(1024)S(1)} all-reduce(f32[1024]{0:T(1024)S(1)} %exponential_reduce_fusion.5), channel_id=1, replica_groups=mesh['src'=16,'tgt'=16] {'tgt'}, use_global_device_ids=true, to_apply=%region_3.0 | all-reduce | flops 1024 | bytes 8192 | tf_op jit(solution)/shard_map/psum | solution.py:13
  76.4 37.2 %pmax.43 = f32[2048]{0:T(1024)S(1)} all-reduce(f32[2048]{0:T(1024)S(1)} %add_reduce_fusion.3), channel_id=1, replica_groups=mesh['src'=16,'tgt'=16] {'src'}, use_global_device_ids=true, to_apply=%region_5.0 | all-reduce | flops 2048 | bytes 16384 | tf_op jit(solution)/shard_map/pmax | solution.py:19
  113.6 4.3 exponential_reduce_fusion.4
  117.9 40.5 %psum.50 = f32[2048]{0:T(1024)S(1)} all-reduce(f32[2048]{0:T(1024)S(1)} %exponential_reduce_fusion.4), channel_id=1, replica_groups=mesh['src'=16,'tgt'=16] {'src'}, use_global_device_ids=true, to_apply=%region_7.0 | all-reduce | flops 2048 | bytes 16384 | tf_op jit(solution)/shard_map/psum | solution.py:20
  158.4 4.0 add_reduce_fusion.2
  162.4 23.6 %pmax.44 = f32[1024]{0:T(1024)S(1)} all-reduce(f32[1024]{0:T(1024)S(1)} %add_reduce_fusion.2), channel_id=1, replica_groups=mesh['src'=16,'tgt'=16] {'tgt'}, use_global_device_ids=true, to_apply=%region_9.0 | all-reduce | flops 1024 | bytes 8192 | tf_op jit(solution)/shard_map/pmax | solution.py:12
  186.0 4.4 exponential_reduce_fusion.3
  190.4 23.6 %psum.51 = f32[1024]{0:T(1024)S(1)} all-reduce(f32[1024]{0:T(1024)S(1)} %exponential_reduce_fusion.3), channel_id=1, replica_groups=mesh['src'=16,'tgt'=16] {'tgt'}, use_global_device_ids=true, to_apply=%region_11.0 | all-reduce | flops 1024 | bytes 8192 | tf_op jit(solution)/shard_map/psum | solution.py:13
  217.9 36.0 %pmax.45 = f32[2048]{0:T(1024)S(1)} all-reduce(f32[2048]{0:T(1024)S(1)} %add_reduce_fusion.1), channel_id=1, replica_groups=mesh['src'=16,'tgt'=16] {'src'}, use_global_device_ids=true, to_apply=%region_13.0 | all-reduce | flops 2048 | bytes 16384 | tf_op jit(solution)/shard_map/pmax | solution.py:19
  253.9 4.3 exponential_reduce_fusion.2
  258.2 38.0 %psum.52 = f32[2048]{0:T(1024)S(1)} all-reduce(f32[2048]{0:T(1024)S(1)} %exponential_reduce_fusion.2), channel_id=1, replica_groups=mesh['src'=16,'tgt'=16] {'src'}, use_global_device_ids=true, to_apply=%region_15.0 | all-reduce | flops 2048 | bytes 16384 | tf_op jit(solution)/shard_map/psum | solution.py:20
  296.2 4.0 add_reduce_fusion
  300.2 23.7 %pmax.46 = f32[1024]{0:T(1024)S(1)} all-reduce(f32[1024]{0:T(1024)S(1)} %add_reduce_fusion), channel_id=1, replica_groups=mesh['src'=16,'tgt'=16] {'tgt'}, use_global_device_ids=true, to_apply=%region_17.0 | all-reduce | flops 1024 | bytes 8192 | tf_op jit(solution)/shard_map/pmax | solution.py:12
  324.0 4.4 exponential_reduce_fusion.1
  328.3 23.6 %psum.53 = f32[1024]{0:T(1024)S(1)} all-reduce(f32[1024]{0:T(1024)S(1)} %exponential_reduce_fusion.1), channel_id=1, replica_groups=mesh['src'=16,'tgt'=16] {'tgt'}, use_global_device_ids=true, to_apply=%region_19.0 | all-reduce | flops 1024 | bytes 8192 | tf_op jit(solution)/shard_map/psum | solution.py:13
  355.9 36.0 %pmax.47 = f32[2048]{0:T(1024)S(1)} all-reduce(f32[2048]{0:T(1024)S(1)} %add_reduce_fusion.4), channel_id=1, replica_groups=mesh['src'=16,'tgt'=16] {'src'}, use_global_device_ids=true, to_apply=%region_21.0 | all-reduce | flops 2048 | bytes 16384 | tf_op jit(solution)/shard_map/pmax | solution.py:19
  391.9 4.3 exponential_reduce_fusion
  396.2 38.0 %psum.54 = f32[2048]{0:T(1024)S(1)} all-reduce(f32[2048]{0:T(1024)S(1)} %exponential_reduce_fusion), channel_id=1, replica_groups=mesh['src'=16,'tgt'=16] {'src'}, use_global_device_ids=true, to_apply=%region_23.0 | all-reduce | flops 2048 | bytes 16384 | tf_op jit(solution)/shard_map/psum | solution.py:20
  434.2 7.0 fusion
  441.3 52.7 %reduce-scatter.2.cloned.1.call-done = f32[64,300]{1,0:T(8,128)} async-done(((f32[1024,300]{1,0:T(8,128)}), f32[64,300]{1,0:T(8,128)}) %reduce-scatter.2.cloned.1.call-update) | async-done | bytes 76816 | tf_op jit(solution)/shard_map/reduce_scatter | solution.py:46
  496.1 257.8 %all-reduce.2.cloned.1.call-done = f32[300,300]{1,0:T(8,128)} async-done(((f32[300,300]{1,0:T(8,128)}), f32[300,300]{1,0:T(8,128)}) %all-reduce.2.cloned.1.call-update) | async-done | bytes 360016 | tf_op jit(solution)/shard_map/psum | solution.py:57
  (26 shorter events, 18.6 us)
Async XLA Ops:
  7.2 2.5 copy-start
  7.2 486.8 %reduce-scatter.2.cloned.1.call-start = ((), (), s32[]{:S(2)}) async-start(), calls=%async_computation.1 | async-start | bytes 1671168 | tf_op jit(solution)/shard_map/reduce_scatter | solution.py:46
  9.7 62.6 %copy-start.3 = (f32[1024]{0:T(1024)S(1)}, f32[1024]{0:T(1024)}, u32[]{:S(2)}) copy-start(f32[1024]{0:T(1024)} %param.8) | copy-start | bytes 12292
  72.4 86.0 %copy-start.1 = (f32[2048]{0:T(1024)S(1)}, f32[2048]{0:T(1024)}, u32[]{:S(2)}) copy-start(f32[2048]{0:T(1024)} %param.9) | copy-start | bytes 24580
  351.9 82.3 %copy-start.2 = (f32[1024]{0:T(1024)}, f32[1024]{0:T(1024)S(1)}, u32[]{:S(2)}) copy-start(f32[1024]{0:T(1024)S(1)} %add_subtract_fusion.3) | copy-start | bytes 12292
  434.2 7.0 copy-start.4
  441.3 312.7 %all-reduce.2.cloned.1.call-start = ((), (), s32[]{:S(2)}) async-start(), calls=%async_computation.2 | async-start | bytes 933888 | tf_op jit(solution)/shard_map/psum | solution.py:57
Sparse Core Ops, SparseCore 0:
  441.4 52.5 reduce-scatter.1
  500.1 253.7 all-reduce.1
where the time goes:
time: 763 us
  blocking collectives  372 us (49%)
  waiting for transfers between devices  311 us (41%)
  other arithmetic  48.2 us (6%)
  matrix products  17.2 us (2%)
  between operations  14.3 us (2%)
    psum x1, waiting for transfers between devices, per_device(): summed = lax.psum(partial_core, ('src', 'tgt'))  258 us
    psum x3, blocking collectives, col_lse(): totals = lax.psum(jnp.sum(jnp.exp(shifted - peaks[None, :]), axis=0), 'src')  116 us
    pmax x3, blocking collectives, col_lse(): peaks = lax.pmax(peaks, 'src')  109 us
    pmax x3, blocking collectives, row_lse(): peaks = lax.pmax(peaks, 'tgt')  76.1 us
    psum x3, blocking collectives, row_lse(): totals = lax.psum(jnp.sum(jnp.exp(shifted - peaks[:, None]), axis=1), 'tgt')  70.7 us
    reduce_scatter x1, waiting for transfers between devices, per_device(): lax.psum_scatter(lax.dot_general(plan, tgt_emb_t, (((1,), (1,)), ((), ())...  52.7 us
  transfers between devices with their start and end apart: 2, of which 2 were waited for; matrix products, arithmetic and copies ran while one was open for 0% of the time, Pallas kernels for 0%

commit v1 on v0

--- a/solution.py
+++ b/solution.py
@@ -10,7 +10,13 @@
 def row_lse(shifted):
     peaks = jnp.max(shifted, axis=1)
     peaks = lax.pmax(peaks, "tgt")
-    totals = lax.psum(jnp.sum(jnp.exp(shifted - peaks[:, None]), axis=1), "tgt")
+
+    def area_create(piece_in, group_axis):
+        u_next = lax.all_gather(piece_in, group_axis)
+        tile_out = jnp.sum(u_next, 0)
+        return tile_out
+
+    totals = area_create(jnp.sum(jnp.exp(shifted - peaks[:, None]), axis=1), "tgt")
     return peaks + jnp.log(totals)
 
 

time: 763 us -> 736 us (0.965)
  blocking collectives: 372 us -> 345 us
    psum x3 -> x0, blocking collectives: 70.7 us -> none  [row_lse(): totals = lax.psum(jnp.sum(jnp.exp(shifted - peaks[:, None]), axis=1), 'tgt')]
    all_gather x0 -> x3, blocking collectives: none -> 43 us  [area_create(): u_next = lax.all_gather(piece_in, group_axis)]
where the time goes in v1:
time: 736 us
  blocking collectives  345 us (47%)
  waiting for transfers between devices  311 us (42%)
  other arithmetic  48.2 us (7%)
  matrix products  17.2 us (2%)
  between operations  14.3 us (2%)
    psum x1, waiting for transfers between devices, per_device(): summed = lax.psum(partial_core, ('src', 'tgt'))  258 us
    psum x3, blocking collectives, col_lse(): totals = lax.psum(jnp.sum(jnp.exp(shifted - peaks[None, :]), axis=0), 'src')  117 us
    pmax x3, blocking collectives, col_lse(): peaks = lax.pmax(peaks, 'src')  109 us
    pmax x3, blocking collectives, row_lse(): peaks = lax.pmax(peaks, 'tgt')  76.1 us
    reduce_scatter x1, waiting for transfers between devices, per_device(): lax.psum_scatter(lax.dot_general(plan, tgt_emb_t, (((1,), (1,)), ((), ())...  53.2 us
    all_gather x3, blocking collectives, area_create(): u_next = lax.all_gather(piece_in, group_axis)  43 us
  transfers between devices with their start and end apart: 2, of which 2 were waited for; matrix products, arithmetic and copies ran while one was open for 0% of the time, Pallas kernels for 0%

profile of v1, /device:TPU:2, one launch (start us, length us, event | category | flops | bytes accessed | tf_op | source)
XLA Modules:
  0.0 735.6 jit_solution(8679277646397729777)
XLA Ops:
  9.7 5.6 fusion.6
  15.4 28.8 %pmax.42 = f32[1024]{0:T(1024)S(1)} all-reduce(f32[1024]{0:T(1024)S(1)} %get-tuple-element.3), channel_id=1, replica_groups=mesh['src'=16,'tgt'=16] {'tgt'}, use_global_device_ids=true, to_apply=%region_1.0 | all-reduce | flops 1024 | bytes 8192 | tf_op jit(solution)/shard_map/pmax | solution.py:12
  44.2 4.6 exponential_reduce_fusion.5
  48.8 14.3 %all-gather = f32[16384]{0:T(1024)S(1)} all-gather(f32[1024]{0:T(1024)S(1)} %exponential_reduce_fusion.5), channel_id=2, replica_groups=mesh['src'=16,'tgt'=16] {'tgt'}, dimensions={0}, use_global_device_ids=true | all-gather | bytes 69632 | tf_op jit(solution)/shard_map/all_gather | solution.py:15
  63.2 4.0 add_reduce_fusion.3
  67.2 37.2 %pmax.43 = f32[2048]{0:T(1024)S(1)} all-reduce(f32[2048]{0:T(1024)S(1)} %add_reduce_fusion.3), channel_id=1, replica_groups=mesh['src'=16,'tgt'=16] {'src'}, use_global_device_ids=true, to_apply=%region_5.0 | all-reduce | flops 2048 | bytes 16384 | tf_op jit(solution)/shard_map/pmax | solution.py:25
  104.4 4.3 exponential_reduce_fusion.4
  108.7 40.5 %psum.28 = f32[2048]{0:T(1024)S(1)} all-reduce(f32[2048]{0:T(1024)S(1)} %exponential_reduce_fusion.4), channel_id=1, replica_groups=mesh['src'=16,'tgt'=16] {'src'}, use_global_device_ids=true, to_apply=%region_7.0 | all-reduce | flops 2048 | bytes 16384 | tf_op jit(solution)/shard_map/psum | solution.py:26
  153.3 23.6 %pmax.44 = f32[1024]{0:T(1024)S(1)} all-reduce(f32[1024]{0:T(1024)S(1)} %add_reduce_fusion.2), channel_id=1, replica_groups=mesh['src'=16,'tgt'=16] {'tgt'}, use_global_device_ids=true, to_apply=%region_9.0 | all-reduce | flops 1024 | bytes 8192 | tf_op jit(solution)/shard_map/pmax | solution.py:12
  176.8 4.4 exponential_reduce_fusion.3
  181.2 14.3 %all-gather.1 = f32[16384]{0:T(1024)S(1)} all-gather(f32[1024]{0:T(1024)S(1)} %exponential_reduce_fusion.3), channel_id=3, replica_groups=mesh['src'=16,'tgt'=16] {'tgt'}, dimensions={0}, use_global_device_ids=true | all-gather | bytes 69632 | tf_op jit(solution)/shard_map/all_gather | solution.py:15
  199.6 35.9 %pmax.45 = f32[2048]{0:T(1024)S(1)} all-reduce(f32[2048]{0:T(1024)S(1)} %add_reduce_fusion.1), channel_id=1, replica_groups=mesh['src'=16,'tgt'=16] {'src'}, use_global_device_ids=true, to_apply=%region_13.0 | all-reduce | flops 2048 | bytes 16384 | tf_op jit(solution)/shard_map/pmax | solution.py:25
  235.5 4.3 exponential_reduce_fusion.2
  239.8 38.0 %psum.29 = f32[2048]{0:T(1024)S(1)} all-reduce(f32[2048]{0:T(1024)S(1)} %exponential_reduce_fusion.2), channel_id=1, replica_groups=mesh['src'=16,'tgt'=16] {'src'}, use_global_device_ids=true, to_apply=%region_15.0 | all-reduce | flops 2048 | bytes 16384 | tf_op jit(solution)/shard_map/psum | solution.py:26
  281.9 23.7 %pmax.46 = f32[1024]{0:T(1024)S(1)} all-reduce(f32[1024]{0:T(1024)S(1)} %add_reduce_fusion), channel_id=1, replica_groups=mesh['src'=16,'tgt'=16] {'tgt'}, use_global_device_ids=true, to_apply=%region_17.0 | all-reduce | flops 1024 | bytes 8192 | tf_op jit(solution)/shard_map/pmax | solution.py:12
  305.6 4.4 exponential_reduce_fusion.1
  310.0 14.3 %all-gather.2 = f32[16384]{0:T(1024)S(1)} all-gather(f32[1024]{0:T(1024)S(1)} %exponential_reduce_fusion.1), channel_id=4, replica_groups=mesh['src'=16,'tgt'=16] {'tgt'}, dimensions={0}, use_global_device_ids=true | all-gather | bytes 69632 | tf_op jit(solution)/shard_map/all_gather | solution.py:15
  324.4 4.0 add_reduce_fusion.4
  328.4 36.0 %pmax.47 = f32[2048]{0:T(1024)S(1)} all-reduce(f32[2048]{0:T(1024)S(1)} %add_reduce_fusion.4), channel_id=1, replica_groups=mesh['src'=16,'tgt'=16] {'src'}, use_global_device_ids=true, to_apply=%region_21.0 | all-reduce | flops 2048 | bytes 16384 | tf_op jit(solution)/shard_map/pmax | solution.py:25
  364.4 4.3 exponential_reduce_fusion
  368.7 38.0 %psum.30 = f32[2048]{0:T(1024)S(1)} all-reduce(f32[2048]{0:T(1024)S(1)} %exponential_reduce_fusion), channel_id=1, replica_groups=mesh['src'=16,'tgt'=16] {'src'}, use_global_device_ids=true, to_apply=%region_23.0 | all-reduce | flops 2048 | bytes 16384 | tf_op jit(solution)/shard_map/psum | solution.py:26
  406.8 7.0 fusion
  413.8 53.2 %reduce-scatter.2.cloned.1.call-done = f32[64,300]{1,0:T(8,128)} async-done(((f32[1024,300]{1,0:T(8,128)}), f32[64,300]{1,0:T(8,128)}) %reduce-scatter.2.cloned.1.call-update) | async-done | bytes 76816 | tf_op jit(solution)/shard_map/reduce_scatter | solution.py:52
  469.2 257.8 %all-reduce.2.cloned.1.call-done = f32[300,300]{1,0:T(8,128)} async-done(((f32[300,300]{1,0:T(8,128)}), f32[300,300]{1,0:T(8,128)}) %all-reduce.2.cloned.1.call-update) | async-done | bytes 360016 | tf_op jit(solution)/shard_map/psum | solution.py:63
  (32 shorter events, 18.7 us)
Async XLA Ops:
  7.2 2.5 copy-start
  7.2 459.9 %reduce-scatter.2.cloned.1.call-start = ((), (), s32[]{:S(2)}) async-start(), calls=%async_computation.1 | async-start | bytes 1671168 | tf_op jit(solution)/shard_map/reduce_scatter | solution.py:52
  9.7 53.5 %copy-start.3 = (f32[1024]{0:T(1024)S(1)}, f32[1024]{0:T(1024)}, u32[]{:S(2)}) copy-start(f32[1024]{0:T(1024)} %param.8) | copy-start | bytes 12292
  63.2 86.1 %copy-start.1 = (f32[2048]{0:T(1024)S(1)}, f32[2048]{0:T(1024)}, u32[]{:S(2)}) copy-start(f32[2048]{0:T(1024)} %param.9) | copy-start | bytes 24580
  324.4 82.4 %copy-start.2 = (f32[1024]{0:T(1024)}, f32[1024]{0:T(1024)S(1)}, u32[]{:S(2)}) copy-start(f32[1024]{0:T(1024)S(1)} %add_subtract_fusion.3) | copy-start | bytes 12292
  406.7 7.0 copy-start.4
  413.8 313.1 %all-reduce.2.cloned.1.call-start = ((), (), s32[]{:S(2)}) async-start(), calls=%async_computation.2 | async-start | bytes 933888 | tf_op jit(solution)/shard_map/psum | solution.py:63
Sparse Core Ops, SparseCore 0:
  413.9 53.0 reduce-scatter.1
  473.1 253.7 all-reduce.1
